TPU v7x, 512 devices: a whole 4x4x16 slice. The times are simulated.
512 devices in a mesh: dp: 16 (over z), owner: 32 (over x, y, core).
Axes of the slice: x: 4, y: 4, z: 16, core: 2. Of those that a mesh axis runs over, the one named last changes fastest.
Arguments:
- tokens: bfloat16 [65536, 8192], P(('dp', 'owner')), may hold values from -6 to 6
- residual: bfloat16 [65536, 8192], P(('dp', 'owner')), may hold values from -6 to 6
- token_adapter_index: int32 [65536, 1], P(('dp', 'owner')), may hold values from 0 to 31; in each aligned block of 128 rows (0 to 127, 128 to 255, ...) at most 6 rows name the same one
- adapter_down_weight: bfloat16 [32, 64, 8192], P('owner', None, 'dp'), may hold values from -0.0625 to 0.0625
- adapter_up_weight: bfloat16 [32, 64, 8192], P('owner', None, 'dp'), may hold values from -0.75 to 0.75
- down_moment_first: bfloat16 [32, 64, 8192], P('owner', None, 'dp'), may hold values from -270 to 270
- down_moment_second: bfloat16 [32, 64, 8192], P('owner', None, 'dp'), may hold values from 816 to 24576
- up_moment_first: bfloat16 [32, 64, 8192], P('owner', None, 'dp'), may hold values from -27.125 to 27.125
- up_moment_second: bfloat16 [32, 64, 8192], P('owner', None, 'dp'), may hold values from 6.125 to 204
Outputs:
- down_update: float32 [32, 64, 8192], P('owner', None, 'dp')
- up_update: float32 [32, 64, 8192], P('owner', None, 'dp')
- token_loss: float32 [65536], P(('dp', 'owner'))
Inputs may be any that keep to these rules, and one draw needn't show every extreme that they name: `token_adapter_index`: of the 128 rows of one device, at most 6 name one adapter, and in some devices one adapter is named by exactly 6.
All inputs are finite; a program needn't handle non-finite values.
Results may differ from a plain program's by a relative error of at most 0.0091.
Values may be sent and summed in bfloat16 or wider, within the bound.
No kernel may reach another device: no remote copies, remote signals or barrier semaphores. Data moves between devices by JAX's collectives and lax.ppermute only.
A program may use at most 128 MiB of HBM per device.

v0:
```python
import jax
import jax.numpy as jnp
from jax import lax
from jax.sharding import PartitionSpec as P

adapter_scale = 0.5
adam_eps = 1e-08


def adam_update(grad, first, second):
    first_new = 0.9 * first.astype(jnp.float32) + 0.1 * grad
    second_new = 0.95 * second.astype(jnp.float32) + 0.05 * grad * grad
    return first_new / (jnp.sqrt(second_new) + adam_eps)


def body(
    tokens,
    residual,
    token_adapter_index,
    adapter_down_weight,
    adapter_up_weight,
    down_moment_first,
    down_moment_second,
    up_moment_first,
    up_moment_second,
):
    owner_index = lax.axis_size("owner")
    tok_rows = tokens.shape[0]
    model_width_value = tokens.shape[1]
    column_span = adapter_down_weight.shape[2]
    slot_capacity = max(2, 3 * tok_rows // (2 * owner_index))
    route_ids = token_adapter_index[:, 0]
    member = (route_ids[:, None] == jnp.arange(owner_index, dtype=jnp.int32)[None, :]).astype(
        jnp.int32
    )
    before = jnp.cumsum(member, axis=0) - member
    within = jnp.sum(before * member, axis=1)
    target = route_ids * slot_capacity + within
    dispatch = (
        jnp.arange(owner_index * slot_capacity, dtype=jnp.int32)[:, None] == target[None, :]
    ).astype(jnp.bfloat16)

    def placed_rows(row_block):
        return jnp.dot(dispatch, row_block, preferred_element_type=jnp.float32).astype(jnp.bfloat16)

    down_full, up_weight_whole = (
        lax.all_gather(adapter_down_weight, "dp", axis=2, tiled=True),
        lax.all_gather(adapter_up_weight, "dp", axis=2, tiled=True),
    )
    down_full = down_full[0]
    up_weight_whole = up_weight_whole[0]

    def spread(row_block):
        return placed_rows(row_block).reshape(owner_index, slot_capacity, model_width_value)

    arrived = lax.all_to_all(
        spread(tokens), "owner", split_axis=0, concat_axis=0, tiled=True
    ).reshape(owner_index * slot_capacity, model_width_value)
    hidden_state = lax.dot_general(
        arrived, down_full, (((1,), (1,)), ((), ())), preferred_element_type=jnp.float32
    ).astype(jnp.bfloat16)
    adapter_output = (
        adapter_scale * jnp.dot(hidden_state, up_weight_whole, preferred_element_type=jnp.float32)
    ).astype(jnp.bfloat16)
    hidden_state, adapter_output = (hidden_state, adapter_output)
    returned = lax.all_to_all(
        adapter_output.reshape(owner_index, slot_capacity, model_width_value),
        "owner",
        split_axis=0,
        concat_axis=0,
        tiled=True,
    )
    returned = returned.reshape(owner_index * slot_capacity, model_width_value)
    adapter_home_index = lax.dot_general(
        dispatch, returned, (((0,), (0,)), ((), ())), preferred_element_type=jnp.float32
    )
    shifted_index = residual.astype(jnp.float32) + adapter_home_index
    token_loss = jnp.mean(0.5 * shifted_index * shifted_index, axis=1)
    output_gradient = lax.all_to_all(
        spread(shifted_index.astype(jnp.bfloat16)), "owner", split_axis=0, concat_axis=0, tiled=True
    )
    output_gradient = output_gradient.reshape(owner_index * slot_capacity, model_width_value)
    up_gradient = adapter_scale * lax.dot_general(
        hidden_state, output_gradient, (((0,), (0,)), ((), ())), preferred_element_type=jnp.float32
    )
    hidden_gradient = (
        adapter_scale
        * lax.dot_general(
            output_gradient,
            up_weight_whole,
            (((1,), (1,)), ((), ())),
            preferred_element_type=jnp.float32,
        )
    ).astype(jnp.bfloat16)
    down_grad = lax.dot_general(
        hidden_gradient, arrived, (((0,), (0,)), ((), ())), preferred_element_type=jnp.float32
    )
    summed_down, summed_up = lax.psum((down_grad, up_gradient), "dp")
    offset = lax.axis_index("dp") * column_span
    down_share = lax.dynamic_slice_in_dim(summed_down, offset, column_span, 1)
    up_share = lax.dynamic_slice_in_dim(summed_up, offset, column_span, 1)
    down_update = adam_update(down_share, down_moment_first[0], down_moment_second[0])
    up_update = adam_update(up_share, up_moment_first[0], up_moment_second[0])
    return (down_update[None], up_update[None], token_loss)


def solution(mesh):
    return jax.shard_map(
        body,
        mesh=mesh,
        in_specs=(
            P(("dp", "owner"), None),
            P(("dp", "owner"), None),
            P(("dp", "owner"), None),
            P("owner", None, "dp"),
            P("owner", None, "dp"),
            P("owner", None, "dp"),
            P("owner", None, "dp"),
            P("owner", None, "dp"),
            P("owner", None, "dp"),
        ),
        out_specs=(P("owner", None, "dp"), P("owner", None, "dp"), P(("dp", "owner"))),
        check_vma=False,
    )
```

profile of v0, /device:TPU:6, one launch (start us, length us, event | category | flops | bytes accessed | tf_op | source)
XLA Modules:
  0.0 467.8 jit_solution(18413843679098739913)
XLA Ops:
  7.9 0.7 fusion.19
  8.8 0.8 select_reduce_fusion
  10.3 2.6 convolution_convert_fusion.1
  12.9 4.9 %reshape.44 = bf16[32,6,8192]{2,1,0:T(8,128)(2,1)} reshape(bf16[192,8192]{1,0:T(8,128)(2,1)} %convolution_convert_fusion.1) | data formatting | bytes 6291456 | tf_op jit(solution)/shard_map/reshape | solution.py:54
  17.8 10.4 %all-to-all-start = ((bf16[32,6,8192]{2,1,0:T(8,128)(2,1)}), bf16[32,6,8192]{2,1,0:T(8,128)(2,1)}, u32[]{:S(2)}, u32[]{:S(2)}) async-start(bf16[32,6,8192]{2,1,0:T(8,128)(2,1)} %reshape.44), calls=%async_computation | async-start | bytes 8388608 | tf_op jit(solution)/shard_map/all_to_all | solution.py:56
  28.3 0.7 all-gather.5.cloned.1.call-update
  29.1 50.0 %all-to-all-done = bf16[32,6,8192]{2,1,0:T(8,128)(2,1)} async-done(((bf16[32,6,8192]{2,1,0:T(8,128)(2,1)}), bf16[32,6,8192]{2,1,0:T(8,128)(2,1)}, u32[]{:S(2)}, u32[]{:S(2)}) %all-to-all-start) | async-done | bytes 3145760 | tf_op jit(solution)/shard_map/all_to_all | solution.py:56
  79.1 4.9 %reshape.45 = bf16[192,8192]{1,0:T(8,128)(2,1)} reshape(bf16[32,6,8192]{2,1,0:T(8,128)(2,1)} %all-to-all-done) | data formatting | bytes 6291456 | tf_op jit(solution)/shard_map/reshape | solution.py:58
  84.0 1.3 all-gather.3.cloned.1.call-done
  85.3 3.3 convolution_convert_fusion.2
  88.6 66.5 %all-gather.5.cloned.1.call-done = bf16[1,64,8192]{2,1,0:T(8,128)(2,1)} async-done(((bf16[1,64,512]{2,1,0:T(8,128)(2,1)}), bf16[1,64,8192]{2,1,0:T(8,128)(2,1)}) %all-gather.5.cloned.1.call-update) | async-done | bytes 1048592 | tf_op jit(solution)/shard_map/all_gather | solution.py:48
  155.0 3.9 fusion
  158.9 4.9 %reshape.46 = bf16[32,6,8192]{2,1,0:T(8,128)(2,1)} reshape(bf16[192,8192]{1,0:T(8,128)(2,1)} %fusion) | data formatting | bytes 6291456 | tf_op jit(solution)/shard_map/reshape | solution.py:67
  163.8 56.6 %all_to_all.15 = bf16[32,6,8192]{2,1,0:T(8,128)(2,1)} all-to-all(bf16[32,6,8192]{2,1,0:T(8,128)(2,1)} %reshape.46), channel_id=1, replica_groups=mesh['dp'=16,'owner'=32] {'owner'}, dimensions={0} | all-to-all | bytes 6291456 | tf_op jit(solution)/shard_map/all_to_all | solution.py:66
  220.4 4.9 %reshape.47 = bf16[192,8192]{1,0:T(8,128)(2,1)} reshape(bf16[32,6,8192]{2,1,0:T(8,128)(2,1)} %all_to_all.15) | data formatting | bytes 6291456 | tf_op jit(solution)/shard_map/reshape | solution.py:73
  225.2 3.9 fusion.1
  229.1 2.6 convolution_convert_fusion
  231.7 4.9 %reshape.48 = bf16[32,6,8192]{2,1,0:T(8,128)(2,1)} reshape(bf16[192,8192]{1,0:T(8,128)(2,1)} %convolution_convert_fusion) | data formatting | bytes 6291456 | tf_op jit(solution)/shard_map/reshape | solution.py:54
  236.6 55.2 %all_to_all.16 = bf16[32,6,8192]{2,1,0:T(8,128)(2,1)} all-to-all(bf16[32,6,8192]{2,1,0:T(8,128)(2,1)} %reshape.48), channel_id=1, replica_groups=mesh['dp'=16,'owner'=32] {'owner'}, dimensions={0} | all-to-all | bytes 6291456 | tf_op jit(solution)/shard_map/all_to_all | solution.py:79
  291.8 4.9 %reshape.49 = bf16[192,8192]{1,0:T(8,128)(2,1)} reshape(bf16[32,6,8192]{2,1,0:T(8,128)(2,1)} %all_to_all.16) | data formatting | bytes 6291456 | tf_op jit(solution)/shard_map/reshape | solution.py:82
  296.7 4.0 convolution_multiply_fusion.1
  300.7 6.5 %fusion.4 = f32[64,8192]{1,0:T(8,128)} fusion(bf16[192,8192]{1,0:T(8,128)(2,1)} %reshape.45, bf16[192,8192]{1,0:T(8,128)(2,1)} %reshape.49, bf16[1,64,8192]{2,1,0:T(8,128)(2,1)S(1)} %copy-done.1), kind=kOutput, calls=%fused_computation.12 | convolution fusion | flops 402677760 | bytes 9437184 | tf_op jit(solution)/shard_map/dot_general | solution.py:95
  307.8 151.6 %all-reduce.3.cloned.1.call-done = (f32[64,8192]{1,0:T(8,128)}, f32[64,8192]{1,0:T(8,128)}) async-done(((f32[64,8192]{1,0:T(8,128)}, f32[64,8192]{1,0:T(8,128)}), (f32[64,8192]{1,0:T(8,128)}, f32[64,8192]{1,0:T(8,128)})) %all-reduce.3.cloned.1.call-update) | async-done | bytes 4194320 | tf_op jit(solution)/shard_map/psum | solution.py:98
  459.4 1.8 fusion.13
  (20 shorter events, 2.2 us)
Async XLA Ops:
  7.2 3.2 copy-start
  7.2 78.1 %all-gather.3.cloned.1.call-start = ((), (), s32[]{:S(2)}) async-start(), calls=%async_computation.3 | async-start | bytes 1114112 | tf_op jit(solution)/shard_map/all_gather | solution.py:47
  17.8 61.2 %all-to-all-start = ((bf16[32,6,8192]{2,1,0:T(8,128)(2,1)}), bf16[32,6,8192]{2,1,0:T(8,128)(2,1)}, u32[]{:S(2)}, u32[]{:S(2)}) async-start(bf16[32,6,8192]{2,1,0:T(8,128)(2,1)} %reshape.44), calls=%async_computation | async-start | bytes 8388608 | tf_op jit(solution)/shard_map/all_to_all | solution.py:56
  28.3 126.8 %all-gather.5.cloned.1.call-start = ((), (), s32[]{:S(2)}) async-start(), calls=%async_computation.4 | async-start | bytes 1114112 | tf_op jit(solution)/shard_map/all_gather | solution.py:48
  29.0 430.4 %all-reduce.3.cloned.1.call-start = ((), (), s32[]{:S(2)}) async-start(), calls=%async_computation.5 | async-start | bytes 8388608 | tf_op jit(solution)/shard_map/psum | solution.py:98
  296.7 4.0 copy-start.1
  307.2 152.2 %copy-start.2 = (bf16[1,64,512]{2,1,0:T(8,128)(2,1)S(1)}, bf16[1,64,512]{2,1,0:T(8,128)(2,1)}, u32[]{:S(2)}) copy-start(bf16[1,64,512]{2,1,0:T(8,128)(2,1)} %param.15) | copy-start | bytes 196612
  307.2 152.2 %copy-start.3 = (bf16[1,64,512]{2,1,0:T(8,128)(2,1)S(1)}, bf16[1,64,512]{2,1,0:T(8,128)(2,1)}, u32[]{:S(2)}) copy-start(bf16[1,64,512]{2,1,0:T(8,128)(2,1)} %param.14) | copy-start | bytes 196612
  307.2 152.2 %copy-start.4 = (bf16[1,64,512]{2,1,0:T(8,128)(2,1)S(1)}, bf16[1,64,512]{2,1,0:T(8,128)(2,1)}, u32[]{:S(2)}) copy-start(bf16[1,64,512]{2,1,0:T(8,128)(2,1)} %param.17) | copy-start | bytes 196612
  307.2 152.2 %copy-start.5 = (bf16[1,64,512]{2,1,0:T(8,128)(2,1)S(1)}, bf16[1,64,512]{2,1,0:T(8,128)(2,1)}, u32[]{:S(2)}) copy-start(bf16[1,64,512]{2,1,0:T(8,128)(2,1)} %param.16) | copy-start | bytes 196612
Sparse Core Ops, SparseCore 0:
  10.1 75.1 all-gather.2
  87.4 67.6 all-gather.4
  307.4 151.9 all-reduce.2
where the time goes:
time: 469 us; the launch traced here: 468 us
  waiting for transfers between devices  271 us (58%)
  blocking collectives  112 us (24%)
  local copies, waits for them, and re-layouts  29.4 us (6%)
  matrix products  26.8 us (6%)
  between operations  13.8 us (3%)
  starting transfers between devices  10.5 us (2%)
  other arithmetic  4.76 us (1%)
    psum x1, waiting for transfers between devices, body(): summed_down, summed_up = lax.psum((down_grad, up_gradient), 'dp')  152 us
    all_gather x1, waiting for transfers between devices, body(): lax.all_gather(adapter_up_weight, 'dp', axis=2, tiled=True)  66.5 us
    all_to_all x1, blocking collectives, body(): lax.all_to_all(adapter_output.reshape(owner_index, slot_capacity, model_w...  56.6 us
    all_to_all x1, blocking collectives, body(): lax.all_to_all(spread(shifted_index.astype(jnp.bfloat16)), 'owner', split...  55.2 us
    all_to_all x1, waiting for transfers between devices, body(): lax.all_to_all(spread(tokens), 'owner', split_axis=0, concat_axis=0, tile...  50 us
    all_to_all x1, starting transfers between devices, body(): lax.all_to_all(spread(tokens), 'owner', split_axis=0, concat_axis=0, tile...  10.4 us
    reshape x2, local copies, waits for them, and re-layouts, spread(): placed_rows(row_block)  9.78 us
  transfers between devices with their start and end apart: 4, of which 4 were waited for; matrix products, arithmetic and copies ran while one was open for 4% of the time, Pallas kernels for 0%

commit v1 on v0

--- a/solution.py
+++ b/solution.py
@@ -2,9 +2,17 @@
 import jax.numpy as jnp
 from jax import lax
 from jax.sharding import PartitionSpec as P
+from jax.lax import axis_index, axis_size, ppermute
 
 adapter_scale = 0.5
 adam_eps = 1e-08
+
+
+def press_terms_over_axis(u_in, ndim_at):
+    val = list(u_in.shape[1:])
+    val[ndim_at] *= u_in.shape[0]
+    carry_in = jnp.moveaxis(u_in, 0, ndim_at).reshape(val)
+    return carry_in
 
 
 def adam_update(grad, first, second):
@@ -24,6 +32,25 @@
     up_moment_first,
     up_moment_second,
 ):
+
+    def heaps_pack(arr_in, a_name, d0):
+        n_chips = axis_size(a_name)
+        rack = tuple(((to_i, (to_i + 1) % n_chips) for to_i in range(n_chips)))
+        all_rows = tuple(((ii, hop_no) for hop_no, ii in rack))
+        then, y = ([], [])
+        for ix in range(n_chips - 1):
+            if ix % 2 == 0:
+                then.append(ppermute(then[-1] if then else arr_in, axis_name=a_name, perm=rack))
+            else:
+                y.append(ppermute(y[-1] if y else arr_in, axis_name=a_name, perm=all_rows))
+        plain = jnp.stack([*then[::-1], arr_in, *y])
+        taken_in = axis_index(a_name)
+        n_now = len(then)
+        all_values = taken_in - n_now
+        plain = plain[(jnp.arange(n_chips) - all_values) % n_chips]
+        local_part = press_terms_over_axis(plain, d0)
+        return local_part
+
     owner_index = lax.axis_size("owner")
     tok_rows = tokens.shape[0]
     model_width_value = tokens.shape[1]
@@ -45,7 +72,7 @@
 
     down_full, up_weight_whole = (
         lax.all_gather(adapter_down_weight, "dp", axis=2, tiled=True),
-        lax.all_gather(adapter_up_weight, "dp", axis=2, tiled=True),
+        heaps_pack(adapter_up_weight, a_name="dp", d0=2),
     )
     down_full = down_full[0]
     up_weight_whole = up_weight_whole[0]

time: 469 us -> 444 us (0.947)
  waiting for transfers between devices: 271 us -> 187 us
  starting transfers between devices: 10.5 us -> 61.8 us
  local copies, waits for them, and re-layouts: 29.4 us -> 36.8 us
    all_gather x1 -> x0, waiting for transfers between devices: 66.5 us -> none  [body(): lax.all_gather(adapter_up_weight, 'dp', axis=2, tiled=True)]
    ppermute x0 -> x15, starting transfers between devices: none -> 53.9 us  [the longest x7 36.5 us: heaps_pack(): y.append(ppermute(y[-1] if y else arr_in, axis_name=a_name, perm=all_rows))]
    all_to_all x1, waiting for transfers between devices: 50 us -> 23 us  [body(): lax.all_to_all(spread(tokens), 'owner', split_axis=0, concat_axis=0, tile...]
    ppermute x0 -> x15, waiting for transfers between devices: none -> 10.6 us  [the longest x8 10.6 us: heaps_pack(): ppermute(then[-1] if then else arr_in, axis_name=a_name, perm=rack)]
    unnamed x12 -> x38, local copies, waits for them, and re-layouts: 0.03 us -> 5.66 us
  transfers between devices with their start and end apart: 4 -> 18, of which waited for: 4 -> 5; matrix products, arithmetic and copies ran while one was open for 4% -> 5% of each run, Pallas kernels for 0% -> 0%
where the time goes in v1:
time: 444 us; the launch traced here: 443 us
  waiting for transfers between devices  187 us (42%)
  blocking collectives  113 us (25%)
  starting transfers between devices  61.8 us (14%)
  local copies, waits for them, and re-layouts  36.8 us (8%)
  matrix products  25.5 us (6%)
  between operations  14.5 us (3%)
  other arithmetic  4.78 us (1%)
    psum x1, waiting for transfers between devices, body(): summed_down, summed_up = lax.psum((down_grad, up_gradient), 'dp')  153 us
    all_to_all x1, blocking collectives, body(): lax.all_to_all(adapter_output.reshape(owner_index, slot_capacity, model_w...  57.5 us
    all_to_all x1, blocking collectives, body(): lax.all_to_all(spread(shifted_index.astype(jnp.bfloat16)), 'owner', split...  55.2 us
    ppermute x7, starting transfers between devices, heaps_pack(): y.append(ppermute(y[-1] if y else arr_in, axis_name=a_name, perm=all_rows))  36.5 us
    all_to_all x1, waiting for transfers between devices, body(): lax.all_to_all(spread(tokens), 'owner', split_axis=0, concat_axis=0, tile...  23 us
    ppermute x8, starting transfers between devices, heaps_pack(): ppermute(then[-1] if then else arr_in, axis_name=a_name, perm=rack)  17.4 us
    ppermute x8, waiting for transfers between devices, heaps_pack(): ppermute(then[-1] if then else arr_in, axis_name=a_name, perm=rack)  10.6 us
    reshape x2, local copies, waits for them, and re-layouts, spread(): placed_rows(row_block)  9.85 us
  transfers between devices with their start and end apart: 18, of which 5 were waited for; matrix products, arithmetic and copies ran while one was open for 5% of the time, Pallas kernels for 0%

profile of v1, /device:TPU:6, one launch (start us, length us, event | category | flops | bytes accessed | tf_op | source)
XLA Modules:
  0.0 442.6 jit_solution(14824861638663987256)
XLA Ops:
  7.2 4.0 collective-permute-start
  11.2 10.0 %collective-permute-done = bf16[1,64,512]{2,1,0:T(8,128)(2,1)S(1)} collective-permute-done((bf16[1,64,512]{2,1,0:T(8,128)(2,1)}, bf16[1,64,512]{2,1,0:T(8,128)(2,1)S(1)}, u32[]{:S(2)}, u32[]{:S(2)}) %collective-permute-start) | collective-permute-done | bytes 65568 | tf_op jit(solution)/shard_map/ppermute | solution.py:43
  23.1 5.1 %collective-permute-start.8 = (bf16[1,64,512]{2,1,0:T(8,128)(2,1)}, bf16[1,64,512]{2,1,0:T(8,128)(2,1)S(1)}, u32[]{:S(2)}, u32[]{:S(2)}) collective-permute-start(bf16[1,64,512]{2,1,0:T(8,128)(2,1)} %param.13), channel_id=1, source_target_pairs={{32,0},{64,32},{96,64},{128,96},{160,128},{192,160},{224,192},{256... | collective-permute-start | bytes 196616 | tf_op jit(solution)/shard_map/ppermute | solution.py:45
  31.4 5.1 %collective-permute-start.9 = (bf16[1,64,512]{2,1,0:T(8,128)(2,1)S(1)}, bf16[1,64,512]{2,1,0:T(8,128)(2,1)S(1)}, u32[]{:S(2)}, u32[]{:S(2)}) collective-permute-start(bf16[1,64,512]{2,1,0:T(8,128)(2,1)S(1)} %collective-permute-done.8), channel_id=1, source_target_pairs={{32,0},{64,32},{96,64},{128,96},{160,128},{192,160},{224,192},{256... | collective-permute-start | bytes 196616 | tf_op jit(solution)/shard_map/ppermute | solution.py:45
  39.3 5.1 %collective-permute-start.10 = (bf16[1,64,512]{2,1,0:T(8,128)(2,1)S(1)}, bf16[1,64,512]{2,1,0:T(8,128)(2,1)S(1)}, u32[]{:S(2)}, u32[]{:S(2)}) collective-permute-start(bf16[1,64,512]{2,1,0:T(8,128)(2,1)S(1)} %collective-permute-done.9), channel_id=1, source_target_pairs={{32,0},{64,32},{96,64},{128,96},{160,128},{192,160},{224,192},{256... | collective-permute-start | bytes 196616 | tf_op jit(solution)/shard_map/ppermute | solution.py:45
  47.1 5.1 %collective-permute-start.11 = (bf16[1,64,512]{2,1,0:T(8,128)(2,1)S(1)}, bf16[1,64,512]{2,1,0:T(8,128)(2,1)S(1)}, u32[]{:S(2)}, u32[]{:S(2)}) collective-permute-start(bf16[1,64,512]{2,1,0:T(8,128)(2,1)S(1)} %collective-permute-done.10), channel_id=1, source_target_pairs={{32,0},{64,32},{96,64},{128,96},{160,128},{192,160},{224,192},{256... | collective-permute-start | bytes 196616 | tf_op jit(solution)/shard_map/ppermute | solution.py:45
  56.8 5.0 %reshape.93 = bf16[32,6,8192]{2,1,0:T(8,128)(2,1)} reshape(bf16[192,8192]{1,0:T(8,128)(2,1)} %convolution_convert_fusion.1) | data formatting | bytes 6291456 | tf_op jit(solution)/shard_map/reshape | solution.py:81
  61.8 7.8 %all-to-all-start = ((bf16[32,6,8192]{2,1,0:T(8,128)(2,1)}), bf16[32,6,8192]{2,1,0:T(8,128)(2,1)}, u32[]{:S(2)}, u32[]{:S(2)}) async-start(bf16[32,6,8192]{2,1,0:T(8,128)(2,1)} %reshape.93), calls=%async_computation | async-start | bytes 8388608 | tf_op jit(solution)/shard_map/all_to_all | solution.py:83
  69.7 5.1 %collective-permute-start.12 = (bf16[1,64,512]{2,1,0:T(8,128)(2,1)S(1)}, bf16[1,64,512]{2,1,0:T(8,128)(2,1)S(1)}, u32[]{:S(2)}, u32[]{:S(2)}) collective-permute-start(bf16[1,64,512]{2,1,0:T(8,128)(2,1)S(1)} %collective-permute-done.11), channel_id=1, source_target_pairs={{32,0},{64,32},{96,64},{128,96},{160,128},{192,160},{224,192},{256... | collective-permute-start | bytes 196616 | tf_op jit(solution)/shard_map/ppermute | solution.py:45
  76.8 5.5 %collective-permute-start.13 = (bf16[1,64,512]{2,1,0:T(8,128)(2,1)S(1)}, bf16[1,64,512]{2,1,0:T(8,128)(2,1)S(1)}, u32[]{:S(2)}, u32[]{:S(2)}) collective-permute-start(bf16[1,64,512]{2,1,0:T(8,128)(2,1)S(1)} %collective-permute-done.12), channel_id=1, source_target_pairs={{32,0},{64,32},{96,64},{128,96},{160,128},{192,160},{224,192},{256... | collective-permute-start | bytes 196616 | tf_op jit(solution)/shard_map/ppermute | solution.py:45
  84.4 5.4 %collective-permute-start.14 = (bf16[1,64,512]{2,1,0:T(8,128)(2,1)S(1)}, bf16[1,64,512]{2,1,0:T(8,128)(2,1)S(1)}, u32[]{:S(2)}, u32[]{:S(2)}) collective-permute-start(bf16[1,64,512]{2,1,0:T(8,128)(2,1)S(1)} %collective-permute-done.13), channel_id=1, source_target_pairs={{32,0},{64,32},{96,64},{128,96},{160,128},{192,160},{224,192},{256... | collective-permute-start | bytes 196616 | tf_op jit(solution)/shard_map/ppermute | solution.py:45
  97.3 23.0 %all-to-all-done = bf16[32,6,8192]{2,1,0:T(8,128)(2,1)} async-done(((bf16[32,6,8192]{2,1,0:T(8,128)(2,1)}), bf16[32,6,8192]{2,1,0:T(8,128)(2,1)}, u32[]{:S(2)}, u32[]{:S(2)}) %all-to-all-start) | async-done | bytes 3145760 | tf_op jit(solution)/shard_map/all_to_all | solution.py:83
  120.3 5.0 %reshape.94 = bf16[192,8192]{1,0:T(8,128)(2,1)} reshape(bf16[32,6,8192]{2,1,0:T(8,128)(2,1)} %all-to-all-done) | data formatting | bytes 6291456 | tf_op jit(solution)/shard_map/reshape | solution.py:85
  125.3 3.3 convolution_convert_fusion.2
  131.3 4.9 %reshape.95 = bf16[32,6,8192]{2,1,0:T(8,128)(2,1)} reshape(bf16[192,8192]{1,0:T(8,128)(2,1)} %fusion) | data formatting | bytes 6291456 | tf_op jit(solution)/shard_map/reshape | solution.py:94
  136.2 57.5 %all_to_all.15 = bf16[32,6,8192]{2,1,0:T(8,128)(2,1)} all-to-all(bf16[32,6,8192]{2,1,0:T(8,128)(2,1)} %reshape.95), channel_id=1, replica_groups=mesh['dp'=16,'owner'=32] {'owner'}, dimensions={0} | all-to-all | bytes 6291456 | tf_op jit(solution)/shard_map/all_to_all | solution.py:93
  193.7 4.9 %reshape.96 = bf16[192,8192]{1,0:T(8,128)(2,1)} reshape(bf16[32,6,8192]{2,1,0:T(8,128)(2,1)} %all_to_all.15) | data formatting | bytes 6291456 | tf_op jit(solution)/shard_map/reshape | solution.py:100
  198.6 3.8 fusion.1
  205.1 4.9 %reshape.97 = bf16[32,6,8192]{2,1,0:T(8,128)(2,1)} reshape(bf16[192,8192]{1,0:T(8,128)(2,1)} %convolution_convert_fusion) | data formatting | bytes 6291456 | tf_op jit(solution)/shard_map/reshape | solution.py:81
  209.9 55.2 %all_to_all.16 = bf16[32,6,8192]{2,1,0:T(8,128)(2,1)} all-to-all(bf16[32,6,8192]{2,1,0:T(8,128)(2,1)} %reshape.97), channel_id=1, replica_groups=mesh['dp'=16,'owner'=32] {'owner'}, dimensions={0} | all-to-all | bytes 6291456 | tf_op jit(solution)/shard_map/all_to_all | solution.py:106
  265.2 4.9 %reshape.98 = bf16[192,8192]{1,0:T(8,128)(2,1)} reshape(bf16[32,6,8192]{2,1,0:T(8,128)(2,1)} %all_to_all.16) | data formatting | bytes 6291456 | tf_op jit(solution)/shard_map/reshape | solution.py:109
  270.0 6.5 %fusion.4 = f32[64,8192]{1,0:T(8,128)} fusion(bf16[192,8192]{1,0:T(8,128)(2,1)} %reshape.94, bf16[192,8192]{1,0:T(8,128)(2,1)} %reshape.98, bf16[64,8192]{1,0:T(8,128)(2,1)S(1)} %bitcast.76), kind=kOutput, calls=%fused_computation.13 | convolution fusion | flops 402677760 | bytes 9437184 | tf_op jit(solution)/shard_map/dot_general | solution.py:122
  276.6 3.9 convolution_multiply_fusion.1
  281.1 152.9 %all-reduce.3.cloned.1.call-done = (f32[64,8192]{1,0:T(8,128)}, f32[64,8192]{1,0:T(8,128)}) async-done(((f32[64,8192]{1,0:T(8,128)}, f32[64,8192]{1,0:T(8,128)}), (f32[64,8192]{1,0:T(8,128)}, f32[64,8192]{1,0:T(8,128)})) %all-reduce.3.cloned.1.call-update) | async-done | bytes 4194320 | tf_op jit(solution)/shard_map/psum | solution.py:125
  (77 shorter events, 34.1 us)
Async XLA Ops:
  7.2 47.0 %copy-start = (bf16[128,8192]{1,0:T(8,128)(2,1)S(1)}, bf16[128,8192]{1,0:T(8,128)(2,1)}, u32[]{:S(2)}) copy-start(bf16[128,8192]{1,0:T(8,128)(2,1)} %param.9) | copy-start | bytes 6291460
  7.2 118.1 %all-gather.2.cloned.1.call-start = ((), (), s32[]{:S(2)}) async-start(), calls=%async_computation.3 | async-start | bytes 1114112 | tf_op jit(solution)/shard_map/all_gather | solution.py:74
  7.2 14.0 %collective-permute-start = (bf16[1,64,512]{2,1,0:T(8,128)(2,1)}, bf16[1,64,512]{2,1,0:T(8,128)(2,1)S(1)}, u32[]{:S(2)}, u32[]{:S(2)}) collective-permute-start(bf16[1,64,512]{2,1,0:T(8,128)(2,1)} %param.13), channel_id=1, source_target_pairs={{0,32},{32,64},{64,96},{96,128},{128,160},{160,192},{192,224},{224... | collective-permute-start | bytes 196616 | tf_op jit(solution)/shard_map/ppermute | solution.py:43
  21.2 7.4 %collective-permute-start.1 = (bf16[1,64,512]{2,1,0:T(8,128)(2,1)S(1)}, bf16[1,64,512]{2,1,0:T(8,128)(2,1)S(1)}, u32[]{:S(2)}, u32[]{:S(2)}) collective-permute-start(bf16[1,64,512]{2,1,0:T(8,128)(2,1)S(1)} %collective-permute-done), channel_id=1, source_target_pairs={{0,32},{32,64},{64,96},{96,128},{128,160},{160,192},{192,224},{224... | collective-permute-start | bytes 196616 | tf_op jit(solution)/shard_map/ppermute | solution.py:43
  23.1 8.3 %collective-permute-start.8 = (bf16[1,64,512]{2,1,0:T(8,128)(2,1)}, bf16[1,64,512]{2,1,0:T(8,128)(2,1)S(1)}, u32[]{:S(2)}, u32[]{:S(2)}) collective-permute-start(bf16[1,64,512]{2,1,0:T(8,128)(2,1)} %param.13), channel_id=1, source_target_pairs={{32,0},{64,32},{96,64},{128,96},{160,128},{192,160},{224,192},{256... | collective-permute-start | bytes 196616 | tf_op jit(solution)/shard_map/ppermute | solution.py:45
  28.6 8.0 %collective-permute-start.2 = (bf16[1,64,512]{2,1,0:T(8,128)(2,1)S(1)}, bf16[1,64,512]{2,1,0:T(8,128)(2,1)S(1)}, u32[]{:S(2)}, u32[]{:S(2)}) collective-permute-start(bf16[1,64,512]{2,1,0:T(8,128)(2,1)S(1)} %collective-permute-done.1), channel_id=1, source_target_pairs={{0,32},{32,64},{64,96},{96,128},{128,160},{160,192},{192,224},{224... | collective-permute-start | bytes 196616 | tf_op jit(solution)/shard_map/ppermute | solution.py:43
  31.4 7.9 %collective-permute-start.9 = (bf16[1,64,512]{2,1,0:T(8,128)(2,1)S(1)}, bf16[1,64,512]{2,1,0:T(8,128)(2,1)S(1)}, u32[]{:S(2)}, u32[]{:S(2)}) collective-permute-start(bf16[1,64,512]{2,1,0:T(8,128)(2,1)S(1)} %collective-permute-done.8), channel_id=1, source_target_pairs={{32,0},{64,32},{96,64},{128,96},{160,128},{192,160},{224,192},{256... | collective-permute-start | bytes 196616 | tf_op jit(solution)/shard_map/ppermute | solution.py:45
  36.6 7.9 %collective-permute-start.3 = (bf16[1,64,512]{2,1,0:T(8,128)(2,1)S(1)}, bf16[1,64,512]{2,1,0:T(8,128)(2,1)S(1)}, u32[]{:S(2)}, u32[]{:S(2)}) collective-permute-start(bf16[1,64,512]{2,1,0:T(8,128)(2,1)S(1)} %collective-permute-done.2), channel_id=1, source_target_pairs={{0,32},{32,64},{64,96},{96,128},{128,160},{160,192},{192,224},{224... | collective-permute-start | bytes 196616 | tf_op jit(solution)/shard_map/ppermute | solution.py:43
  39.3 7.8 %collective-permute-start.10 = (bf16[1,64,512]{2,1,0:T(8,128)(2,1)S(1)}, bf16[1,64,512]{2,1,0:T(8,128)(2,1)S(1)}, u32[]{:S(2)}, u32[]{:S(2)}) collective-permute-start(bf16[1,64,512]{2,1,0:T(8,128)(2,1)S(1)} %collective-permute-done.9), channel_id=1, source_target_pairs={{32,0},{64,32},{96,64},{128,96},{160,128},{192,160},{224,192},{256... | collective-permute-start | bytes 196616 | tf_op jit(solution)/shard_map/ppermute | solution.py:45
  44.5 7.7 %collective-permute-start.4 = (bf16[1,64,512]{2,1,0:T(8,128)(2,1)S(1)}, bf16[1,64,512]{2,1,0:T(8,128)(2,1)S(1)}, u32[]{:S(2)}, u32[]{:S(2)}) collective-permute-start(bf16[1,64,512]{2,1,0:T(8,128)(2,1)S(1)} %collective-permute-done.3), channel_id=1, source_target_pairs={{0,32},{32,64},{64,96},{96,128},{128,160},{160,192},{192,224},{224... | collective-permute-start | bytes 196616 | tf_op jit(solution)/shard_map/ppermute | solution.py:43
  47.1 22.6 %collective-permute-start.11 = (bf16[1,64,512]{2,1,0:T(8,128)(2,1)S(1)}, bf16[1,64,512]{2,1,0:T(8,128)(2,1)S(1)}, u32[]{:S(2)}, u32[]{:S(2)}) collective-permute-start(bf16[1,64,512]{2,1,0:T(8,128)(2,1)S(1)} %collective-permute-done.10), channel_id=1, source_target_pairs={{32,0},{64,32},{96,64},{128,96},{160,128},{192,160},{224,192},{256... | collective-permute-start | bytes 196616 | tf_op jit(solution)/shard_map/ppermute | solution.py:45
  52.2 22.6 %collective-permute-start.5 = (bf16[1,64,512]{2,1,0:T(8,128)(2,1)S(1)}, bf16[1,64,512]{2,1,0:T(8,128)(2,1)S(1)}, u32[]{:S(2)}, u32[]{:S(2)}) collective-permute-start(bf16[1,64,512]{2,1,0:T(8,128)(2,1)S(1)} %collective-permute-done.4), channel_id=1, source_target_pairs={{0,32},{32,64},{64,96},{96,128},{128,160},{160,192},{192,224},{224... | collective-permute-start | bytes 196616 | tf_op jit(solution)/shard_map/ppermute | solution.py:43
  61.8 30.7 %copy-start.1 = (bf16[1,64,512]{2,1,0:T(8,128)(2,1)S(1)}, bf16[1,64,512]{2,1,0:T(8,128)(2,1)}, u32[]{:S(2)}) copy-start(bf16[1,64,512]{2,1,0:T(8,128)(2,1)} %param.13) | copy-start | bytes 196612
  61.8 58.6 %all-to-all-start = ((bf16[32,6,8192]{2,1,0:T(8,128)(2,1)}), bf16[32,6,8192]{2,1,0:T(8,128)(2,1)}, u32[]{:S(2)}, u32[]{:S(2)}) async-start(bf16[32,6,8192]{2,1,0:T(8,128)(2,1)} %reshape.93), calls=%async_computation | async-start | bytes 8388608 | tf_op jit(solution)/shard_map/all_to_all | solution.py:83
  69.6 364.4 %all-reduce.3.cloned.1.call-start = ((), (), s32[]{:S(2)}) async-start(), calls=%async_computation.4 | async-start | bytes 8388608 | tf_op jit(solution)/shard_map/psum | solution.py:125
  69.7 7.1 %collective-permute-start.12 = (bf16[1,64,512]{2,1,0:T(8,128)(2,1)S(1)}, bf16[1,64,512]{2,1,0:T(8,128)(2,1)S(1)}, u32[]{:S(2)}, u32[]{:S(2)}) collective-permute-start(bf16[1,64,512]{2,1,0:T(8,128)(2,1)S(1)} %collective-permute-done.11), channel_id=1, source_target_pairs={{32,0},{64,32},{96,64},{128,96},{160,128},{192,160},{224,192},{256... | collective-permute-start | bytes 196616 | tf_op jit(solution)/shard_map/ppermute | solution.py:45
  74.8 7.6 %collective-permute-start.6 = (bf16[1,64,512]{2,1,0:T(8,128)(2,1)S(1)}, bf16[1,64,512]{2,1,0:T(8,128)(2,1)S(1)}, u32[]{:S(2)}, u32[]{:S(2)}) collective-permute-start(bf16[1,64,512]{2,1,0:T(8,128)(2,1)S(1)} %collective-permute-done.5), channel_id=1, source_target_pairs={{0,32},{32,64},{64,96},{96,128},{128,160},{160,192},{192,224},{224... | collective-permute-start | bytes 196616 | tf_op jit(solution)/shard_map/ppermute | solution.py:43
  76.8 7.6 %collective-permute-start.13 = (bf16[1,64,512]{2,1,0:T(8,128)(2,1)S(1)}, bf16[1,64,512]{2,1,0:T(8,128)(2,1)S(1)}, u32[]{:S(2)}, u32[]{:S(2)}) collective-permute-start(bf16[1,64,512]{2,1,0:T(8,128)(2,1)S(1)} %collective-permute-done.12), channel_id=1, source_target_pairs={{32,0},{64,32},{96,64},{128,96},{160,128},{192,160},{224,192},{256... | collective-permute-start | bytes 196616 | tf_op jit(solution)/shard_map/ppermute | solution.py:45
  82.5 7.4 %collective-permute-start.7 = (bf16[1,64,512]{2,1,0:T(8,128)(2,1)S(1)}, bf16[1,64,512]{2,1,0:T(8,128)(2,1)S(1)}, u32[]{:S(2)}, u32[]{:S(2)}) collective-permute-start(bf16[1,64,512]{2,1,0:T(8,128)(2,1)S(1)} %collective-permute-done.6), channel_id=1, source_target_pairs={{0,32},{32,64},{64,96},{96,128},{128,160},{160,192},{192,224},{224... | collective-permute-start | bytes 196616 | tf_op jit(solution)/shard_map/ppermute | solution.py:43
  84.4 9.9 %collective-permute-start.14 = (bf16[1,64,512]{2,1,0:T(8,128)(2,1)S(1)}, bf16[1,64,512]{2,1,0:T(8,128)(2,1)S(1)}, u32[]{:S(2)}, u32[]{:S(2)}) collective-permute-start(bf16[1,64,512]{2,1,0:T(8,128)(2,1)S(1)} %collective-permute-done.13), channel_id=1, source_target_pairs={{32,0},{64,32},{96,64},{128,96},{160,128},{192,160},{224,192},{256... | collective-permute-start | bytes 196616 | tf_op jit(solution)/shard_map/ppermute | solution.py:45
  280.5 153.4 %copy-start.7 = (bf16[1,64,512]{2,1,0:T(8,128)(2,1)S(1)}, bf16[1,64,512]{2,1,0:T(8,128)(2,1)}, u32[]{:S(2)}) copy-start(bf16[1,64,512]{2,1,0:T(8,128)(2,1)} %param.15) | copy-start | bytes 196612
  280.5 153.4 %copy-start.8 = (bf16[1,64,512]{2,1,0:T(8,128)(2,1)S(1)}, bf16[1,64,512]{2,1,0:T(8,128)(2,1)}, u32[]{:S(2)}) copy-start(bf16[1,64,512]{2,1,0:T(8,128)(2,1)} %param.14) | copy-start | bytes 196612
  280.5 153.4 %copy-start.9 = (bf16[1,64,512]{2,1,0:T(8,128)(2,1)S(1)}, bf16[1,64,512]{2,1,0:T(8,128)(2,1)}, u32[]{:S(2)}) copy-start(bf16[1,64,512]{2,1,0:T(8,128)(2,1)} %param.17) | copy-start | bytes 196612
  280.5 153.4 %copy-start.10 = (bf16[1,64,512]{2,1,0:T(8,128)(2,1)S(1)}, bf16[1,64,512]{2,1,0:T(8,128)(2,1)}, u32[]{:S(2)}) copy-start(bf16[1,64,512]{2,1,0:T(8,128)(2,1)} %param.16) | copy-start | bytes 196612
  (5 other events, 76.7 us)
Sparse Core Ops, SparseCore 0:
  28.4 69.3 all-gather.1
  280.7 153.2 all-reduce.2
